TPU v7x, 256 devices: a whole 4x4x8 slice. The times are simulated.
256 devices in a mesh: dp: 64 (over y, z, core), vocab: 4 (over x).
Axes of the slice: x: 4, y: 4, z: 8, core: 2. Of those that a mesh axis runs over, the one named last changes fastest.
Arguments:
- hidden_rows: bfloat16 [16384, 5120], P('dp'), may hold values from -300 to 300, as said below
- plan_lengths: int32 [64], replicated, may hold values from 1 to 256, 8192 in all
- shard_of_class: int32 [64], replicated, may hold values from 0 to 63, each once
- head_weight: bfloat16 [5120, 3072], P(None, 'vocab'), may hold values from -0.078125 to 0.078125
- teacher_logprobs: bfloat16 [8192, 3072], P('dp', 'vocab'), as said below
Outputs:
- row_grad: bfloat16 [16384, 5120], P('dp')
- row_kl: float32 [8192], P('dp')
Inputs may be any that keep to these rules, and one draw needn't show every extreme that they name: `plan_lengths`: the plan lengths sum to 8192 and the longest is exactly 256. `shard_of_class`: each shard is named once. `hidden_rows`: unused slots hold finite values. `teacher_logprobs`: each row is a log-softmax over the 3072 entries, rounded to bfloat16.
All inputs are finite; a program needn't handle non-finite values.
Results may differ from a plain program's by a relative error of at most 0.0046.
Values may be sent and summed in bfloat16 or wider, within the bound.
No kernel may reach another device: no remote copies, remote signals or barrier semaphores. Data moves between devices by JAX's collectives and lax.ppermute only.
A program may use at most 64 MiB of HBM per device.

v0:
```python
import jax
import jax.numpy as jnp
from jax import lax
from jax.sharding import PartitionSpec as P

loss_scale = 64.0


def divergence(row_block, teacher_block, live_rows, weight):
    logits = jnp.dot(row_block, weight, preferred_element_type=jnp.float32)
    log_teacher = teacher_block.astype(jnp.float32)
    teacher_prob = jnp.exp(log_teacher)
    own_top = jnp.max(logits, axis=1)
    own_mass = jnp.sum(teacher_prob, axis=1)
    own_cross = jnp.sum(teacher_prob * (log_teacher - logits), axis=1)
    row_top = lax.pmax(own_top, "vocab")
    own_total = jnp.sum(jnp.exp(logits - row_top[:, None]), axis=1)
    exp_total, prob_total, cross_term = lax.psum((own_total, own_mass, own_cross), "vocab")
    log_total = row_top + jnp.log(exp_total)
    row_div = (cross_term + prob_total * log_total) * live_rows
    grad_logits = (
        loss_scale
        * (prob_total[:, None] * jnp.exp(logits - log_total[:, None]) - teacher_prob)
        * live_rows[:, None]
    ).astype(jnp.bfloat16)
    partial_grad = lax.dot_general(
        grad_logits, weight, (((1,), (1,)), ((), ())), preferred_element_type=jnp.float32
    )
    hidden_grad = lax.psum(partial_grad, "vocab").astype(jnp.bfloat16)
    return (hidden_grad, row_div)


def body(hidden_rows, plan_lengths, shard_of_class, head_weight, teacher_logprobs):
    shards = lax.axis_size("dp")
    myself = lax.axis_index("dp")
    source_slots = hidden_rows.shape[0]
    feature_width = hidden_rows.shape[1]
    slot_depth = source_slots // shards
    balanced = teacher_logprobs.shape[0]
    offsets = jnp.cumsum(plan_lengths) - plan_lengths
    classes = jnp.arange(shards, dtype=jnp.int32)
    inverse = jnp.sum(
        jnp.where(shard_of_class[None, :] == classes[:, None], classes[None, :], 0), axis=1
    )
    own_offset = offsets[myself]
    column_of = (inverse - own_offset) % shards
    shard_at = shard_of_class[(own_offset + classes) % shards]
    rank_rows = jnp.arange(slot_depth, dtype=jnp.int32)[:, None]
    recv_row = rank_rows * shards + ((inverse[myself] - offsets) % shards)[None, :]
    recv_live = recv_row < plan_lengths[None, :]
    recv_slot = jnp.where(recv_live, (offsets[None, :] + recv_row) // shards, balanced)
    safe_slot = jnp.minimum(recv_slot, balanced - 1).reshape(-1)
    outgoing = jnp.take(hidden_rows.reshape(slot_depth, shards, feature_width), column_of, axis=1)
    arriving = lax.all_to_all(outgoing, "dp", split_axis=1, concat_axis=1, tiled=True)
    flattened = arriving.reshape(slot_depth * shards, feature_width)
    live_rows = recv_live.reshape(-1).astype(jnp.float32)
    teacher_slots = jnp.take(teacher_logprobs, safe_slot, axis=0)
    returning, row_div = divergence(flattened, teacher_slots, live_rows, head_weight)
    row_kl = jnp.zeros((balanced,), jnp.float32).at[recv_slot.reshape(-1)].add(row_div, mode="drop")
    share_width = returning.shape[1]
    returned = lax.all_to_all(
        returning.reshape(slot_depth, shards, share_width),
        "dp",
        split_axis=1,
        concat_axis=1,
        tiled=True,
    )
    grad_share = jnp.take(returned, shard_at, axis=1).reshape(source_slots, share_width)
    return (grad_share, row_kl)


def solution(mesh):
    return jax.shard_map(
        body,
        mesh=mesh,
        in_specs=(P("dp", None), P(), P(), P(None, "vocab"), P("dp", "vocab")),
        out_specs=(P("dp", None), P("dp")),
        check_vma=False,
    )
```

profile of v0, /device:TPU:1, one launch (start us, length us, event | category | flops | bytes accessed | tf_op | source)
XLA Modules:
  0.0 298.8 jit_solution(14799237197427120690)
XLA Ops:
  0.6 0.8 select_reduce_fusion
  1.5 0.8 copy.15
  2.2 0.1 reduce-window.9
  2.3 0.1 reduce
  2.4 0.6 dynamic_slice.6
  3.0 1.3 and_select_fusion.4
  4.3 0.6 dynamic_slice.7
  4.9 0.7 compare_and_fusion.1
  5.6 3.8 %copy.16 = bf16[4,64,5120]{2,0,1:T(4,128)(2,1)S(1)} copy(bf16[4,64,5120]{2,1,0:T(8,128)(2,1)} %bitcast.18) | data formatting | bytes 5242880 | tf_op jit(solution)/shard_map/reshape | solution.py:53
  9.3 4.2 %gather_fusion.2 = bf16[64,4,5120]{2,1,0:T(4,128)(2,1)} fusion(bf16[4,64,5120]{2,0,1:T(4,128)(2,1)S(1)} %copy.16, s32[1024]{0:T(1024)S(1)} %pad_clamp_fusion.1), kind=kCustom, calls=%fused_computation.clone | custom fusion | bytes 5243136 | tf_op jit(solution)/shard_map/jit(_take)/gather | solution.py:53
  13.5 4.5 %select_bitcast_fusion.1 = bf16[4,64,5120]{2,0,1:T(4,128)(2,1)} fusion(bf16[64,4,5120]{2,1,0:T(4,128)(2,1)} %gather_fusion.2, pred[64]{0:T(512)(128)(4,1)S(1)} %get-tuple-element.14), kind=kLoop, calls=%fused_computation.6 | loop fusion | flops 1310720 | bytes 5242944 | tf_op jit(solution)/shard_map/jit(_take)/select_n | solution.py:53
  18.0 13.3 %all-to-all-start = ((bf16[4,64,5120]{2,0,1:T(4,128)(2,1)}), bf16[4,64,5120]{2,0,1:T(4,128)(2,1)S(1)}, u32[]{:S(2)}, u32[]{:S(2)}) async-start(bf16[4,64,5120]{2,0,1:T(4,128)(2,1)} %select_bitcast_fusion.1), calls=%async_computation | async-start | bytes 5242880 | tf_op jit(solution)/shard_map/all_to_all | solution.py:54
  31.4 0.1 add.183
  31.6 0.1 lt.100
  31.8 1.2 gather_fusion
  33.1 60.5 %all-to-all-done = bf16[4,64,5120]{2,0,1:T(4,128)(2,1)S(1)} async-done(((bf16[4,64,5120]{2,0,1:T(4,128)(2,1)}), bf16[4,64,5120]{2,0,1:T(4,128)(2,1)S(1)}, u32[]{:S(2)}, u32[]{:S(2)}) %all-to-all-start) | async-done | bytes 2621472 | tf_op jit(solution)/shard_map/all_to_all | solution.py:54
  93.5 0.8 copy.17
  94.3 5.5 %fusion.19 = (f32[256]{0:T(256)S(1)}, f32[256,768]{1,0:T(8,128)S(1)}) fusion(bf16[256,5120]{1,0:T(8,128)(2,1)S(1)} %bitcast.21, bf16[5120,768]{1,0:T(8,128)(2,1)} %param.10), kind=kOutput, calls=%fused_computation.66 | convolution fusion | flops 2013462272 | bytes 11273216 | tf_op jit(solution)/shard_map/dot_general | solution.py:10
  99.9 8.5 %pmax.7 = f32[256]{0:T(256)S(1)} all-reduce(f32[256]{0:T(256)S(1)} %get-tuple-element.16), channel_id=1, replica_groups=mesh['dp'=64,'vocab'=4] {'vocab'}, use_global_device_ids=true, to_apply=%region_5.7 | all-reduce | flops 256 | bytes 2048 | tf_op jit(solution)/shard_map/pmax | solution.py:16
  108.3 0.6 fusion.5
  108.9 6.2 %all-reduce.1 = (f32[256]{0:T(256)S(1)}, f32[256]{0:T(256)S(1)}) all-reduce(f32[256]{0:T(256)S(1)} %get-tuple-element.4, f32[256]{0:T(256)S(1)} %get-tuple-element.5), channel_id=1, replica_groups=mesh['dp'=64,'vocab'=4] {'vocab'}, use_global_device_ids=true, to_apply=%region_7.9 | all-reduce | flops 512 | bytes 4096 | tf_op jit(solution)/shard_map/psum | solution.py:18
  115.1 8.0 %fusion.6 = f32[256,5120]{1,0:T(8,128)} fusion(bf16[5120,768]{1,0:T(8,128)(2,1)} %param.10, f32[256,768]{1,0:T(8,128)S(1)} %get-tuple-element.17, f32[256]{0:T(256)S(1)} %broadcast_select_fusion.1, f32[256]{0:T(256)S(1)} %log_add_fusion, f32[256]{0:T(256)S(1)} %get-tuple-element.9, bf16[256,768]{1,0:T(8,128)(2,1)S(1)} %gather_fusion, ...), kind=kOutput, calls=%fused_computation.16 | convolution fusion | flops 2014642176 | bytes 14290176 | tf_op jit(solution)/shard_map/dot_general | solution.py:26
  123.1 89.4 %all-reduce.3 = (bf16[256,5120]{1,0:T(8,128)(2,1)S(1)}, f32[256]{0:T(256)S(1)}) all-reduce(f32[256,5120]{1,0:T(8,128)} %fusion.6, f32[256]{0:T(256)S(1)} %get-tuple-element.3), channel_id=1, replica_groups=mesh['dp'=64,'vocab'=4] {'vocab'}, use_global_device_ids=true, to_apply=%region_8.10 | all-reduce | flops 1310976 | bytes 7866368 | tf_op jit(solution)/shard_map/psum | solution.py:29
  212.5 3.5 %copy.18 = bf16[4,64,5120]{2,0,1:T(4,128)(2,1)} copy(bf16[4,64,5120]{2,1,0:T(8,128)(2,1)S(1)} %bitcast.20) | data formatting | bytes 5242880 | tf_op jit(solution)/shard_map/reshape | solution.py:62
  216.0 11.2 %all-to-all-start.1 = ((bf16[4,64,5120]{2,0,1:T(4,128)(2,1)}), bf16[4,64,5120]{2,0,1:T(4,128)(2,1)S(1)}, u32[]{:S(2)}, u32[]{:S(2)}) async-start(bf16[4,64,5120]{2,0,1:T(4,128)(2,1)} %copy.18), calls=%async_computation.1 | async-start | bytes 5242880 | tf_op jit(solution)/shard_map/all_to_all | solution.py:61
  227.1 0.7 fusion.15
  227.8 0.8 gather_fusion.1
  228.6 2.8 scatter_custom_fusion
  231.5 57.9 %all-to-all-done.1 = bf16[4,64,5120]{2,0,1:T(4,128)(2,1)S(1)} async-done(((bf16[4,64,5120]{2,0,1:T(4,128)(2,1)}), bf16[4,64,5120]{2,0,1:T(4,128)(2,1)S(1)}, u32[]{:S(2)}, u32[]{:S(2)}) %all-to-all-start.1) | async-done | bytes 2621472 | tf_op jit(solution)/shard_map/all_to_all | solution.py:61
  289.4 4.2 %gather_fusion.3 = bf16[64,4,5120]{2,1,0:T(4,128)(2,1)} fusion(bf16[4,64,5120]{2,0,1:T(4,128)(2,1)S(1)} %all-to-all-done.1, s32[1024]{0:T(1024)S(1)} %pad_clamp_fusion), kind=kCustom, calls=%fused_computation.1.clone | custom fusion | bytes 5243136 | tf_op jit(solution)/shard_map/jit(_take)/gather | solution.py:68
  293.5 3.0 %select_bitcast_fusion = bf16[4,64,5120]{2,0,1:T(4,128)(2,1)S(1)} fusion(bf16[64,4,5120]{2,1,0:T(4,128)(2,1)} %gather_fusion.3, pred[64]{0:T(512)(128)(4,1)S(1)} %compare_and_fusion), kind=kLoop, calls=%fused_computation.5 | loop fusion | flops 1310720 | bytes 5242944 | tf_op jit(solution)/shard_map/jit(_take)/select_n | solution.py:68
  296.5 2.3 copy.19
  (23 shorter events, 0.4 us)
Async XLA Ops:
  0.6 31.2 %copy-start = (bf16[128,768]{1,0:T(8,128)(2,1)S(1)}, bf16[128,768]{1,0:T(8,128)(2,1)}, u32[]{:S(2)}) copy-start(bf16[128,768]{1,0:T(8,128)(2,1)} %param.11) | copy-start | bytes 589828
  18.0 13.5 %copy-start.2 = (s32[64]{0:T(128)S(1)}, s32[64]{0:T(128)}, u32[]{:S(2)}) copy-start(s32[64]{0:T(128)} %param.8) | copy-start | bytes 772
  18.0 75.5 %all-to-all-start = ((bf16[4,64,5120]{2,0,1:T(4,128)(2,1)}), bf16[4,64,5120]{2,0,1:T(4,128)(2,1)S(1)}, u32[]{:S(2)}, u32[]{:S(2)}) async-start(bf16[4,64,5120]{2,0,1:T(4,128)(2,1)} %select_bitcast_fusion.1), calls=%async_computation | async-start | bytes 5242880 | tf_op jit(solution)/shard_map/all_to_all | solution.py:54
  216.0 11.8 %copy-start.1 = (s32[64]{0:T(128)S(1)}, s32[64]{0:T(128)}, u32[]{:S(2)}) copy-start(s32[64]{0:T(128)} %param.9) | copy-start | bytes 772
  216.0 73.4 %all-to-all-start.1 = ((bf16[4,64,5120]{2,0,1:T(4,128)(2,1)}), bf16[4,64,5120]{2,0,1:T(4,128)(2,1)S(1)}, u32[]{:S(2)}, u32[]{:S(2)}) async-start(bf16[4,64,5120]{2,0,1:T(4,128)(2,1)} %copy.18), calls=%async_computation.1 | async-start | bytes 5242880 | tf_op jit(solution)/shard_map/all_to_all | solution.py:61
where the time goes:
time: 299 us
  waiting for transfers between devices  118 us (39%)
  blocking collectives  104 us (35%)
  starting transfers between devices  24.4 us (8%)
  local copies, waits for them, and re-layouts  22.9 us (8%)
  other arithmetic  14.8 us (5%)
  matrix products  13.5 us (5%)
    psum x1, blocking collectives, divergence(): hidden_grad = lax.psum(partial_grad, 'vocab').astype(jnp.bfloat16)  89.4 us
    all_to_all x1, waiting for transfers between devices, body(): lax.all_to_all(outgoing, 'dp', split_axis=1, concat_axis=1, tiled=True)  60.5 us
    all_to_all x1, waiting for transfers between devices, body(): lax.all_to_all(returning.reshape(slot_depth, shards, share_width), 'dp',...  57.9 us
    all_to_all x1, starting transfers between devices, body(): lax.all_to_all(outgoing, 'dp', split_axis=1, concat_axis=1, tiled=True)  13.3 us
    all_to_all x1, starting transfers between devices, body(): lax.all_to_all(returning.reshape(slot_depth, shards, share_width), 'dp',...  11.2 us
    pmax x1, blocking collectives, divergence(): row_top = lax.pmax(own_top, 'vocab')  8.47 us
    dot_general x1, matrix products, divergence(): lax.dot_general(grad_logits, weight, (((1,), (1,)), ((), ())), preferred_...  7.99 us
    psum x1, blocking collectives, divergence(): lax.psum((own_total, own_mass, own_cross), 'vocab')  6.18 us
  transfers between devices with their start and end apart: 2, of which 2 were waited for; matrix products, arithmetic and copies ran while one was open for 2% of the time, Pallas kernels for 0%

commit v1 on v0

--- a/solution.py
+++ b/solution.py
@@ -51,7 +51,10 @@
     recv_slot = jnp.where(recv_live, (offsets[None, :] + recv_row) // shards, balanced)
     safe_slot = jnp.minimum(recv_slot, balanced - 1).reshape(-1)
     outgoing = jnp.take(hidden_rows.reshape(slot_depth, shards, feature_width), column_of, axis=1)
-    arriving = lax.all_to_all(outgoing, "dp", split_axis=1, concat_axis=1, tiled=True)
+    arriving = jnp.concatenate(
+        lax.all_to_all(jnp.stack(jnp.split(outgoing, lax.axis_size("dp"), axis=1)), "dp", 0, 0),
+        axis=1,
+    )
     flattened = arriving.reshape(slot_depth * shards, feature_width)
     live_rows = recv_live.reshape(-1).astype(jnp.float32)
     teacher_slots = jnp.take(teacher_logprobs, safe_slot, axis=0)

time: 299 us -> 339 us (1.13)
  local copies, waits for them, and re-layouts: 22.9 us -> 63.4 us
    unnamed x6 -> x69, local copies, waits for them, and re-layouts: 0.02 us -> 39.8 us
where the time goes in v1:
time: 339 us; the launch traced here: 338 us
  waiting for transfers between devices  119 us (35%)
  blocking collectives  104 us (31%)
  local copies, waits for them, and re-layouts  63.4 us (19%)
  starting transfers between devices  24.4 us (7%)
  matrix products  13.5 us (4%)
  other arithmetic  13.3 us (4%)
    psum x1, blocking collectives, divergence(): hidden_grad = lax.psum(partial_grad, 'vocab').astype(jnp.bfloat16)  89.4 us
    all_to_all x1, waiting for transfers between devices, body(): lax.all_to_all(jnp.stack(jnp.split(outgoing, lax.axis_size('dp'), axis=1)...  60.4 us
    all_to_all x1, waiting for transfers between devices, body(): lax.all_to_all(returning.reshape(slot_depth, shards, share_width), 'dp',...  58.6 us
    unnamed x69, local copies, waits for them, and re-layouts  39.8 us
    all_to_all x1, starting transfers between devices, body(): lax.all_to_all(jnp.stack(jnp.split(outgoing, lax.axis_size('dp'), axis=1)...  13.3 us
    all_to_all x1, starting transfers between devices, body(): lax.all_to_all(returning.reshape(slot_depth, shards, share_width), 'dp',...  11.1 us
    pmax x1, blocking collectives, divergence(): row_top = lax.pmax(own_top, 'vocab')  8.47 us
    dot_general x1, matrix products, divergence(): lax.dot_general(grad_logits, weight, (((1,), (1,)), ((), ())), preferred_...  8 us
  transfers between devices with their start and end apart: 2, of which 2 were waited for; matrix products, arithmetic and copies ran while one was open for 2% of the time, Pallas kernels for 0%

profile of v1, /device:TPU:1, one launch (start us, length us, event | category | flops | bytes accessed | tf_op | source)
XLA Modules:
  0.0 338.3 jit_solution(16366928813156998381)
XLA Ops:
  0.6 0.8 select_reduce_fusion
  1.5 0.8 copy.79
  3.0 1.3 and_select_fusion.4
  4.9 0.7 compare_and_fusion.1
  5.6 0.7 fusion.15
  6.2 3.8 %copy.80 = bf16[4,64,5120]{2,0,1:T(4,128)(2,1)S(1)} copy(bf16[4,64,5120]{2,1,0:T(8,128)(2,1)} %bitcast.276) | data formatting | bytes 5242880 | tf_op jit(solution)/shard_map/reshape | solution.py:53
  10.0 4.2 %gather_fusion.2 = bf16[64,4,5120]{2,1,0:T(4,128)(2,1)} fusion(bf16[4,64,5120]{2,0,1:T(4,128)(2,1)S(1)} %copy.80, s32[1024]{0:T(1024)S(1)} %get-tuple-element.18), kind=kCustom, calls=%fused_computation.clone | custom fusion | bytes 5243136 | tf_op jit(solution)/shard_map/jit(_take)/gather | solution.py:53
  14.2 3.0 select_bitcast_fusion.1
  17.2 0.6 constant_dynamic-update-slice_fusion.63
  20.3 0.6 constant_dynamic-update-slice_fusion.58
  23.5 0.6 constant_dynamic-update-slice_fusion.53
  24.8 0.6 constant_dynamic-update-slice_fusion.51
  27.9 0.6 constant_dynamic-update-slice_fusion.46
  29.2 0.6 constant_dynamic-update-slice_fusion.44
  32.4 0.6 constant_dynamic-update-slice_fusion.39
  57.7 13.3 %all-to-all-start = ((bf16[64,4,1,5120]{3,1,2,0:T(4,128)(2,1)}), bf16[64,4,1,5120]{3,1,2,0:T(4,128)(2,1)S(1)}, u32[]{:S(2)}, u32[]{:S(2)}) async-start(bf16[64,4,1,5120]{3,1,2,0:T(4,128)(2,1)} %constant_dynamic-update-slice_fusion), calls=%async_computation | async-start | bytes 5242880 | tf_op jit(solution)/shard_map/all_to_all | solution.py:55
  71.5 1.2 gather_fusion
  72.7 60.4 %all-to-all-done = bf16[64,4,1,5120]{3,1,2,0:T(4,128)(2,1)S(1)} async-done(((bf16[64,4,1,5120]{3,1,2,0:T(4,128)(2,1)}), bf16[64,4,1,5120]{3,1,2,0:T(4,128)(2,1)S(1)}, u32[]{:S(2)}, u32[]{:S(2)}) %all-to-all-start) | async-done | bytes 2621472 | tf_op jit(solution)/shard_map/all_to_all | solution.py:55
  133.2 0.8 copy.81
  134.0 5.5 %fusion.19 = (f32[256]{0:T(256)S(1)}, f32[256,768]{1,0:T(8,128)S(1)}) fusion(bf16[256,5120]{1,0:T(8,128)(2,1)S(1)} %bitcast.279, bf16[5120,768]{1,0:T(8,128)(2,1)} %param.10), kind=kOutput, calls=%fused_computation.194 | convolution fusion | flops 2013462272 | bytes 11273216 | tf_op jit(solution)/shard_map/dot_general | solution.py:10
  139.5 8.5 %pmax.7 = f32[256]{0:T(256)S(1)} all-reduce(f32[256]{0:T(256)S(1)} %get-tuple-element.16), channel_id=1, replica_groups=mesh['dp'=64,'vocab'=4] {'vocab'}, use_global_device_ids=true, to_apply=%region_5.7 | all-reduce | flops 256 | bytes 2048 | tf_op jit(solution)/shard_map/pmax | solution.py:16
  148.6 6.0 %all-reduce.1 = (f32[256]{0:T(256)S(1)}, f32[256]{0:T(256)S(1)}) all-reduce(f32[256]{0:T(256)S(1)} %get-tuple-element.4, f32[256]{0:T(256)S(1)} %get-tuple-element.5), channel_id=1, replica_groups=mesh['dp'=64,'vocab'=4] {'vocab'}, use_global_device_ids=true, to_apply=%region_7.9 | all-reduce | flops 512 | bytes 4096 | tf_op jit(solution)/shard_map/psum | solution.py:18
  154.6 8.0 %fusion.6 = f32[256,5120]{1,0:T(8,128)} fusion(bf16[5120,768]{1,0:T(8,128)(2,1)} %param.10, f32[256,768]{1,0:T(8,128)S(1)} %get-tuple-element.17, f32[256]{0:T(256)S(1)} %broadcast_select_fusion.1, f32[256]{0:T(256)S(1)} %log_add_fusion, f32[256]{0:T(256)S(1)} %get-tuple-element.9, bf16[256,768]{1,0:T(8,128)(2,1)S(1)} %gather_fusion, ...), kind=kOutput, calls=%fused_computation.16 | convolution fusion | flops 2014642176 | bytes 14290176 | tf_op jit(solution)/shard_map/dot_general | solution.py:26
  162.6 89.4 %all-reduce.3 = (bf16[256,5120]{1,0:T(8,128)(2,1)S(1)}, f32[256]{0:T(256)S(1)}) all-reduce(f32[256,5120]{1,0:T(8,128)} %fusion.6, f32[256]{0:T(256)S(1)} %get-tuple-element.3), channel_id=1, replica_groups=mesh['dp'=64,'vocab'=4] {'vocab'}, use_global_device_ids=true, to_apply=%region_8.10 | all-reduce | flops 1310976 | bytes 7866368 | tf_op jit(solution)/shard_map/psum | solution.py:29
  252.0 3.5 %copy.82 = bf16[4,64,5120]{2,0,1:T(4,128)(2,1)} copy(bf16[4,64,5120]{2,1,0:T(8,128)(2,1)S(1)} %bitcast.278) | data formatting | bytes 5242880 | tf_op jit(solution)/shard_map/reshape | solution.py:65
  255.5 11.1 %all-to-all-start.1 = ((bf16[4,64,5120]{2,0,1:T(4,128)(2,1)}), bf16[4,64,5120]{2,0,1:T(4,128)(2,1)S(1)}, u32[]{:S(2)}, u32[]{:S(2)}) async-start(bf16[4,64,5120]{2,0,1:T(4,128)(2,1)} %copy.82), calls=%async_computation.1 | async-start | bytes 5242880 | tf_op jit(solution)/shard_map/all_to_all | solution.py:64
  266.6 0.8 gather_fusion.1
  267.5 2.8 scatter_custom_fusion
  270.3 58.6 %all-to-all-done.1 = bf16[4,64,5120]{2,0,1:T(4,128)(2,1)S(1)} async-done(((bf16[4,64,5120]{2,0,1:T(4,128)(2,1)}), bf16[4,64,5120]{2,0,1:T(4,128)(2,1)S(1)}, u32[]{:S(2)}, u32[]{:S(2)}) %all-to-all-start.1) | async-done | bytes 2621472 | tf_op jit(solution)/shard_map/all_to_all | solution.py:64
  328.9 4.2 %gather_fusion.3 = bf16[64,4,5120]{2,1,0:T(4,128)(2,1)} fusion(bf16[4,64,5120]{2,0,1:T(4,128)(2,1)S(1)} %all-to-all-done.1, s32[1024]{0:T(1024)S(1)} %pad_clamp_fusion), kind=kCustom, calls=%fused_computation.1.clone | custom fusion | bytes 5243136 | tf_op jit(solution)/shard_map/jit(_take)/gather | solution.py:71
  333.0 3.0 select_bitcast_fusion
  336.0 2.3 copy.83
  (86 shorter events, 38.6 us)
Async XLA Ops:
  0.6 70.9 %copy-start = (bf16[128,768]{1,0:T(8,128)(2,1)S(1)}, bf16[128,768]{1,0:T(8,128)(2,1)}, u32[]{:S(2)}) copy-start(bf16[128,768]{1,0:T(8,128)(2,1)} %param.11) | copy-start | bytes 589828
  57.7 13.5 %copy-start.2 = (s32[64]{0:T(128)S(1)}, s32[64]{0:T(128)}, u32[]{:S(2)}) copy-start(s32[64]{0:T(128)} %param.8) | copy-start | bytes 772
  57.7 75.5 %all-to-all-start = ((bf16[64,4,1,5120]{3,1,2,0:T(4,128)(2,1)}), bf16[64,4,1,5120]{3,1,2,0:T(4,128)(2,1)S(1)}, u32[]{:S(2)}, u32[]{:S(2)}) async-start(bf16[64,4,1,5120]{3,1,2,0:T(4,128)(2,1)} %constant_dynamic-update-slice_fusion), calls=%async_computation | async-start | bytes 5242880 | tf_op jit(solution)/shard_map/all_to_all | solution.py:55
  255.5 11.1 %copy-start.1 = (s32[64]{0:T(128)S(1)}, s32[64]{0:T(128)}, u32[]{:S(2)}) copy-start(s32[64]{0:T(128)} %param.9) | copy-start | bytes 772
  255.5 73.4 %all-to-all-start.1 = ((bf16[4,64,5120]{2,0,1:T(4,128)(2,1)}), bf16[4,64,5120]{2,0,1:T(4,128)(2,1)S(1)}, u32[]{:S(2)}, u32[]{:S(2)}) async-start(bf16[4,64,5120]{2,0,1:T(4,128)(2,1)} %copy.82), calls=%async_computation.1 | async-start | bytes 5242880 | tf_op jit(solution)/shard_map/all_to_all | solution.py:64
